TPU v7x, 512 devices: a whole 4x8x8 slice. The times are simulated.
512 devices in a mesh: section: 8 (over z), kv: 64 (over x, y, core).
Axes of the slice: x: 4, y: 8, z: 8, core: 2. Of those that a mesh axis runs over, the one named last changes fastest.
Arguments:
- held: bfloat16 [8, 128, 8192], P('section', None, 'kv'), may hold values from -6 to 6
- fresh: bfloat16 [1, 128, 8192], P(None, None, 'kv'), may hold values from -6 to 6
- block_starts: int32 [8], replicated, may hold values from 12288 to 24576
- fresh_starts: int32 [1], replicated, may hold values from 12288 to 24576
- norm_gain: float32 [8, 8192], P('section'), may hold values from 0.25 to 1.75
- w_qkv: bfloat16 [8, 8192, 5120], P('section', None, 'kv'), may hold values from -0.0625 to 0.0625
- w_out: bfloat16 [8, 4096, 8192], P('section', None, 'kv'), may hold values from -12 to 12
- cache_keys: bfloat16 [8, 24576, 512], P('section', 'kv'), may hold values from -400 to 400
- cache_values: bfloat16 [8, 24576, 512], P('section', 'kv'), may hold values from -6 to 6
- cache_lengths: int32 [8, 64], P('section', 'kv'), may hold values from 96 to 384, as said below
Outputs:
- produced: bfloat16 [8, 2, 128, 8192], P('section', None, None, 'kv')
Inputs may be any that keep to these rules, and one draw needn't show every extreme that they name: `cache_lengths`: each section has one block filled to 384.
All inputs are finite; a program needn't handle non-finite values.
Results may differ from a plain program's by a relative error of at most 0.017.
The roundings to bfloat16 on the way count: a program that leaves them out, or rounds other values in their place, can miss the bound.
Values may be sent and summed in bfloat16 or wider, within the bound.
No kernel may reach another device: no remote copies, remote signals or barrier semaphores. Data moves between devices by JAX's collectives and lax.ppermute only.
A program may use at most 128 MiB of HBM per device.

v0:
```python
import jax
import jax.numpy as jnp
from jax import lax
from jax.sharding import PartitionSpec as P

HD = 128
HEADS_Q = 32
KV_HEADS = 4


def passed_along(block, axis, distance):
    devices = range(lax.axis_size(axis))
    route = [(i - distance, i) for i in devices if i - distance in devices]
    return lax.ppermute(block, axis, route)


def block_partial(query, key_rows, value_rows, valid):
    row_count = query.shape[0]
    head_count = query.shape[1]
    head_width = query.shape[2]
    group_count = key_rows.shape[1]
    group_size = head_count // group_count
    shaped = jnp.transpose(
        query.reshape(row_count, group_count, group_size, head_width), (1, 0, 2, 3)
    )
    key_major = jnp.transpose(key_rows, (1, 0, 2))
    value_major = jnp.transpose(value_rows, (1, 0, 2))
    allowed = valid[:, None, :]

    def one_group(packed):
        group_query, group_keys, group_values = packed
        scores = jnp.einsum(
            "tgd,id->tgi", group_query, group_keys, preferred_element_type=jnp.float32
        ) * head_width ** (-0.5)
        row_max = jnp.max(jnp.where(allowed, scores, -1e30), axis=2)
        expo = jnp.where(allowed, jnp.exp(scores - row_max[..., None]), 0.0)
        row_sum = jnp.sum(expo, axis=2)
        weights = expo.astype(jnp.bfloat16)
        weighted = jnp.einsum(
            "tgi,id->tgd", weights, group_values, preferred_element_type=jnp.float32
        )
        return (row_max, row_sum, weighted)

    maxima, totals, sums = lax.map(one_group, (shaped, key_major, value_major))
    maxima = jnp.transpose(maxima, (1, 0, 2)).reshape(row_count, head_count)
    totals = jnp.transpose(totals, (1, 0, 2)).reshape(row_count, head_count)
    sums = jnp.transpose(sums, (1, 0, 2, 3)).reshape(row_count, head_count * head_width)
    return (maxima, totals, sums)


def combine_two(left_part, right_part):
    head_count = left_part[0].shape[1]
    row_count = left_part[0].shape[0]
    overall = jnp.maximum(left_part[0], right_part[0])
    left_factor = jnp.exp(left_part[0] - overall)
    right_factor = jnp.exp(right_part[0] - overall)
    total = left_part[1] * left_factor + right_part[1] * right_factor
    left_sum = left_part[2].reshape(row_count, head_count, -1) * left_factor[..., None]
    right_sum = right_part[2].reshape(row_count, head_count, -1) * right_factor[..., None]
    return (overall, total, (left_sum + right_sum).reshape(row_count, -1))


def merge_stack(maxima, totals, sums):
    count = maxima.shape[0]
    row_count = maxima.shape[1]
    head_count = maxima.shape[2]
    overall = jnp.max(maxima, axis=0)
    factor = jnp.exp(maxima - overall)
    total = jnp.sum(totals * factor, axis=0)
    summed = jnp.sum(sums.reshape(count, row_count, head_count, -1) * factor[..., None], axis=0)
    return (summed / total[..., None]).reshape(row_count, -1).astype(jnp.bfloat16)


def on_device(
    held,
    fresh,
    block_starts,
    fresh_starts,
    norm_gain,
    w_qkv,
    w_out,
    cache_keys,
    cache_values,
    cache_lengths,
):
    kv_index = lax.axis_index("kv")
    section_index = lax.axis_index("section")
    tick_count = fresh.shape[0] + 1
    row_count = held.shape[1]
    slot_count = cache_keys.shape[1]
    key_rows = cache_keys[0].reshape(slot_count, KV_HEADS, HD)
    value_rows = cache_values[0].reshape(slot_count, KV_HEADS, HD)
    filled = cache_lengths[0, 0]
    gain = norm_gain[0]
    weight_in = w_qkv[0]
    weight_out = w_out[0]
    slot_ids = jnp.arange(slot_count, dtype=jnp.int32)
    positions = kv_index * slot_count + slot_ids
    row_ids = jnp.arange(row_count, dtype=jnp.int32)
    causal = row_ids[None, :] <= row_ids[:, None]
    current = held[0]
    results = []
    for tick_index in range(tick_count):
        if tick_index > 0:
            passed = passed_along(current, "section", 1)
            current = jnp.where(section_index == 0, fresh[tick_index - 1], passed)
        anchor = section_index - tick_index
        start = jnp.where(
            anchor >= 0,
            block_starts[jnp.maximum(anchor, 0)],
            fresh_starts[jnp.clip(-anchor - 1, 0, tick_count - 2)],
        )
        gathered = lax.all_gather(current, "kv", axis=1, tiled=True)
        wide = gathered.astype(jnp.float32)
        normed = (
            wide * lax.rsqrt(jnp.mean(wide * wide, axis=1, keepdims=True) + 1e-05) * gain
        ).astype(jnp.bfloat16)
        local_cols = jnp.dot(normed, weight_in, preferred_element_type=jnp.float32).astype(
            jnp.bfloat16
        )
        united = lax.all_gather(local_cols, "kv", axis=1, tiled=True)
        query = united[:, : HEADS_Q * HD].reshape(row_count, HEADS_Q, HD)
        new_keys = united[:, HEADS_Q * HD : (HEADS_Q + KV_HEADS) * HD].reshape(
            row_count, KV_HEADS, HD
        )
        new_values = united[:, (HEADS_Q + KV_HEADS) * HD :].reshape(row_count, KV_HEADS, HD)
        usable = (slot_ids < filled) & (positions < start)
        valid = jnp.broadcast_to(usable[None, :], (row_count, slot_count))
        partial_value = block_partial(query, key_rows, value_rows, valid)

        def with_own(parts):
            return combine_two(parts, block_partial(query, new_keys, new_values, causal))

        def without_own(parts):
            return parts

        partial_value = lax.cond(kv_index == 0, with_own, without_own, partial_value)
        received = (
            lax.all_to_all(partial_value[0][None], "kv", split_axis=1, concat_axis=0, tiled=True),
            lax.all_to_all(partial_value[1][None], "kv", split_axis=1, concat_axis=0, tiled=True),
            lax.all_to_all(partial_value[2][None], "kv", split_axis=1, concat_axis=0, tiled=True),
        )
        attended = merge_stack(received[0], received[1], received[2])
        branch = jnp.dot(
            lax.all_gather(attended, "kv", axis=0, tiled=True),
            weight_out,
            preferred_element_type=jnp.float32,
        )
        current = (current.astype(jnp.float32) + branch).astype(jnp.bfloat16)
        results.append(current)
    return jnp.stack(results, 0)[None]


def solution(mesh):
    in_specs = (
        P("section", None, "kv"),
        P(None, None, "kv"),
        P(),
        P(),
        P("section", None),
        P("section", None, "kv"),
        P("section", None, "kv"),
        P("section", "kv", None),
        P("section", "kv", None),
        P("section", "kv"),
    )
    out_specs = P("section", None, None, "kv")
    return jax.shard_map(
        on_device, mesh=mesh, in_specs=in_specs, out_specs=out_specs, check_vma=False
    )
```

profile of v0, /device:TPU:1, one launch (start us, length us, event | category | flops | bytes accessed | tf_op | source)
XLA Modules:
  0.0 792.7 jit_solution(17048475888363732458)
XLA Ops:
  7.3 86.4 %all-gather.16.cloned.1.call-done = bf16[1,128,8192]{2,1,0:T(8,128)(2,1)} async-done(((bf16[1,128,128]{2,1,0:T(8,128)(2,1)}), bf16[1,128,8192]{2,1,0:T(8,128)(2,1)}) %all-gather.16.cloned.1.call-update) | async-done | bytes 2097168 | tf_op jit(solution)/shard_map/all_gather | solution.py:113
  93.7 2.2 fusion.77
  103.6 75.6 %all-gather.10.cloned.1.call-done = bf16[128,5120]{0,1:T(8,128)(2,1)} async-done(((bf16[128,80]{0,1:T(8,128)(2,1)}), bf16[128,5120]{0,1:T(8,128)(2,1)}) %all-gather.10.cloned.1.call-update) | async-done | bytes 1310736 | tf_op jit(solution)/shard_map/all_gather | solution.py:121
  182.1 13.5 %while.58 = (s32[]{:T(128)}, f32[4,128,8]{1,2,0:T(8,128)S(1)}, f32[4,128,8]{1,2,0:T(8,128)S(1)}, f32[4,128,8,128]{3,1,2,0:T(8,128)S(1)}, bf16[4,128,8,128]{3,1,2...) while((s32[]{:T(128)}, f32[4,128,8]{1,2,0:T(8,128)S(1)}, ...), condition=%wide.region_4.5_spmd.clone, body=%wide.region_1.4_spmd.clone.sunk | while | flops 204863488 | bytes 5737833 | solution.py:44
  195.6 12.1 %conditional.2 = (f32[128,32]{0,1:T(8,128)S(1)}, f32[128,32]{0,1:T(8,128)S(1)}, f32[128,4096]{1,0:T(8,128)}) conditional(s32[]{:T(128)} %convert_element_type.53, (f32[128,4,8,128]{3,0,2,1:T(8,128)S(1)}, f32[128,32]{0,1:T(8,128)S(1)}, f32[128,32]{0,1:T(8,128)S(1)}) %tuple.192, (bf16[128,4096]{0,1:T(8,128)(2,1)}, bf16[128,5120]{0,1:T(8,128)(2,1)}, ...), branch_computations={%region_5.6_spmd, %region_6.11_spmd} | conditional | flops 69883904 | bytes 51759524 | solution.py:137
  196.8 3.0 copy.131
  208.4 25.7 %all-to-all-start.2 = ((f32[1,128,32]{2,0,1:T(1,128)}), f32[1,128,32]{2,0,1:T(1,128)S(1)}, u32[]{:S(2)}, u32[]{:S(2)}) async-start(f32[1,128,32]{2,0,1:T(1,128)} %bitcast.73), calls=%async_computation.2 | async-start | bytes 131072 | tf_op jit(solution)/shard_map/all_to_all | solution.py:140
  234.8 9.2 %all-to-all-done.2 = f32[1,128,32]{2,0,1:T(1,128)S(1)} async-done(((f32[1,128,32]{2,0,1:T(1,128)}), f32[1,128,32]{2,0,1:T(1,128)S(1)}, u32[]{:S(2)}, u32[]{:S(2)}) %all-to-all-start.2) | async-done | bytes 16416 | tf_op jit(solution)/shard_map/all_to_all | solution.py:140
  244.0 4.4 all-to-all-start.1
  248.4 5.3 broadcast_in_dim.169
  253.8 4.5 all-to-all-done.1
  258.3 5.9 all-to-all-start
  265.9 49.5 %all-to-all-done = f32[1,128,4096]{2,0,1:T(1,128)S(1)} async-done(((f32[1,128,4096]{2,0,1:T(1,128)}), f32[1,128,4096]{2,0,1:T(1,128)S(1)}, u32[]{:S(2)}, u32[]{:S(2)}) %all-to-all-start) | async-done | bytes 2097184 | tf_op jit(solution)/shard_map/all_to_all | solution.py:141
  316.0 4.3 multiply_reduce_fusion.1
  321.1 79.2 %all-gather.18.cloned.1.call-done = bf16[64,2,4096]{2,1,0:T(2,128)(2,1)} async-done(((bf16[1,2,4096]{2,1,0:T(2,128)(2,1)}), bf16[64,2,4096]{2,1,0:T(2,128)(2,1)}) %all-gather.18.cloned.1.call-update) | async-done | bytes 1048592 | tf_op jit(solution)/shard_map/all_gather | solution.py:145
  402.2 3.3 collective-permute-start
  407.3 78.1 %all-gather.12.cloned.1.call-done = bf16[128,8192]{1,0:T(8,128)(2,1)} async-done(((bf16[128,128]{1,0:T(8,128)(2,1)}), bf16[128,8192]{1,0:T(8,128)(2,1)}) %all-gather.12.cloned.1.call-update) | async-done | bytes 2097168 | tf_op jit(solution)/shard_map/all_gather | solution.py:113
  485.5 2.2 fusion.74
  487.7 1.6 fusion.92
  489.4 81.6 %all-gather.14.cloned.1.call-done = bf16[128,5120]{0,1:T(8,128)(2,1)} async-done(((bf16[128,80]{0,1:T(8,128)(2,1)}), bf16[128,5120]{0,1:T(8,128)(2,1)}) %all-gather.14.cloned.1.call-update) | async-done | bytes 1310736 | tf_op jit(solution)/shard_map/all_gather | solution.py:121
  573.9 13.5 %while.59 = (s32[]{:T(128)}, f32[4,128,8]{1,2,0:T(8,128)S(1)}, f32[4,128,8]{1,2,0:T(8,128)S(1)}, f32[4,128,8,128]{3,1,2,0:T(8,128)S(1)}, bf16[4,128,8,128]{3,1,2...) while((s32[]{:T(128)}, f32[4,128,8]{1,2,0:T(8,128)S(1)}, ...), condition=%wide.region_18.19_spmd.clone, body=%wide.region_15.18_spmd.clone.sunk | while | flops 204863488 | bytes 5737833 | solution.py:44
  587.4 4.4 conditional.3
  588.6 3.0 copy.132
  592.5 24.2 %all-to-all-start.5 = ((f32[1,128,32]{2,0,1:T(1,128)}), f32[1,128,32]{2,0,1:T(1,128)S(1)}, u32[]{:S(2)}, u32[]{:S(2)}) async-start(f32[1,128,32]{2,0,1:T(1,128)} %bitcast.95), calls=%async_computation.5 | async-start | bytes 131072 | tf_op jit(solution)/shard_map/all_to_all | solution.py:140
  617.4 9.2 %all-to-all-done.5 = f32[1,128,32]{2,0,1:T(1,128)S(1)} async-done(((f32[1,128,32]{2,0,1:T(1,128)}), f32[1,128,32]{2,0,1:T(1,128)S(1)}, u32[]{:S(2)}, u32[]{:S(2)}) %all-to-all-start.5) | async-done | bytes 16416 | tf_op jit(solution)/shard_map/all_to_all | solution.py:140
  626.6 4.4 all-to-all-start.4
  631.0 5.3 broadcast_in_dim.172
  636.3 4.5 all-to-all-done.4
  640.9 5.9 all-to-all-start.3
  647.1 50.9 %all-to-all-done.3 = f32[1,128,4096]{2,0,1:T(1,128)S(1)} async-done(((f32[1,128,4096]{2,0,1:T(1,128)}), f32[1,128,4096]{2,0,1:T(1,128)S(1)}, u32[]{:S(2)}, u32[]{:S(2)}) %all-to-all-start.3) | async-done | bytes 2097184 | tf_op jit(solution)/shard_map/all_to_all | solution.py:141
  698.6 4.3 multiply_reduce_fusion
  703.6 79.3 %all-gather.20.cloned.1.call-done = bf16[64,2,4096]{2,1,0:T(2,128)(2,1)} async-done(((bf16[1,2,4096]{2,1,0:T(2,128)(2,1)}), bf16[64,2,4096]{2,1,0:T(2,128)(2,1)}) %all-gather.20.cloned.1.call-update) | async-done | bytes 1048592 | tf_op jit(solution)/shard_map/all_gather | solution.py:145
  (125 shorter events, 54.5 us)
Async XLA Ops:
  6.5 89.4 %copy-start = (bf16[1,8192,80]{1,2,0:T(8,128)(2,1)S(1)}, bf16[1,8192,80]{1,2,0:T(8,128)(2,1)}, u32[]{:S(2)}) copy-start(bf16[1,8192,80]{1,2,0:T(8,128)(2,1)} %param.27) | copy-start | bytes 3932164
  6.5 89.4 %copy-start.27 = (f32[1,8192]{1,0:T(1,128)S(1)}, f32[1,8192]{1,0:T(1,128)}, u32[]{:S(2)}) copy-start(f32[1,8192]{1,0:T(1,128)} %param.26) | copy-start | bytes 98308
  6.5 87.1 %all-gather.16.cloned.1.call-start = ((), (), s32[]{:S(2)}) async-start(), calls=%async_computation.9 | async-start | bytes 2129920 | tf_op jit(solution)/shard_map/all_gather | solution.py:113
  7.3 172.0 %all-gather.10.cloned.1.call-start = ((), (), s32[]{:S(2)}) async-start(), calls=%async_computation.6 | async-start | bytes 1331200 | tf_op jit(solution)/shard_map/all_gather | solution.py:121
  93.7 2.3 copy-start.9
  95.9 1.7 copy-start.13
  95.9 2.9 copy-start.14
  97.6 3.7 copy-start.26
  180.5 1.3 copy-start.2
  208.4 35.6 %all-to-all-start.2 = ((f32[1,128,32]{2,0,1:T(1,128)}), f32[1,128,32]{2,0,1:T(1,128)S(1)}, u32[]{:S(2)}, u32[]{:S(2)}) async-start(f32[1,128,32]{2,0,1:T(1,128)} %bitcast.73), calls=%async_computation.2 | async-start | bytes 131072 | tf_op jit(solution)/shard_map/all_to_all | solution.py:140
  244.0 9.8 %copy-start.16 = (f32[1,128,32]{2,0,1:T(1,128)}, f32[1,128,32]{2,0,1:T(1,128)S(1)}, u32[]{:S(2)}) copy-start(f32[1,128,32]{2,0,1:T(1,128)S(1)} %all-to-all-done.2) | copy-start | bytes 49156
  244.0 14.3 %all-to-all-start.1 = ((f32[1,128,32]{2,0,1:T(1,128)}), f32[1,128,32]{2,0,1:T(1,128)S(1)}, u32[]{:S(2)}, u32[]{:S(2)}) async-start(f32[1,128,32]{2,0,1:T(1,128)} %bitcast.70), calls=%async_computation.1 | async-start | bytes 131072 | tf_op jit(solution)/shard_map/all_to_all | solution.py:139
  258.3 57.1 %all-to-all-start = ((f32[1,128,4096]{2,0,1:T(1,128)}), f32[1,128,4096]{2,0,1:T(1,128)S(1)}, u32[]{:S(2)}, u32[]{:S(2)}) async-start(f32[1,128,4096]{2,0,1:T(1,128)} %broadcast_in_dim.169), calls=%async_computation | async-start | bytes 4194304 | tf_op jit(solution)/shard_map/all_to_all | solution.py:141
  264.2 136.0 %all-gather.18.cloned.1.call-start = ((), (), s32[]{:S(2)}) async-start(), calls=%async_computation.10 | async-start | bytes 1064960 | tf_op jit(solution)/shard_map/all_gather | solution.py:145
  320.3 81.4 %copy-start.7 = (bf16[1,4096,128]{2,1,0:T(8,128)(2,1)S(1)}, bf16[1,4096,128]{2,1,0:T(8,128)(2,1)}, u32[]{:S(2)}) copy-start(bf16[1,4096,128]{2,1,0:T(8,128)(2,1)} %param.28) | copy-start | bytes 3145732
  320.3 81.4 %copy-start.21 = (bf16[1,128,128]{2,1,0:T(8,128)(2,1)S(1)}, bf16[1,128,128]{2,1,0:T(8,128)(2,1)}, u32[]{:S(2)}) copy-start(bf16[1,128,128]{2,1,0:T(8,128)(2,1)} %param.22) | copy-start | bytes 98308
  321.0 85.5 %copy-start.25 = (bf16[1,128,128]{2,1,0:T(8,128)(2,1)S(1)}, bf16[1,128,128]{2,1,0:T(8,128)(2,1)}, u32[]{:S(2)}) copy-start(bf16[1,128,128]{2,1,0:T(8,128)(2,1)} %param.23) | copy-start | bytes 98308
  321.0 164.5 %all-gather.12.cloned.1.call-start = ((), (), s32[]{:S(2)}) async-start(), calls=%async_computation.7 | async-start | bytes 2129920 | tf_op jit(solution)/shard_map/all_gather | solution.py:113
  401.7 86.0 %copy-start.28 = (f32[1,8192]{1,0:T(1,128)S(1)}, f32[1,8192]{1,0:T(1,128)}, u32[]{:S(2)}) copy-start(f32[1,8192]{1,0:T(1,128)} %param.26) | copy-start | bytes 98308
  402.2 87.2 %copy-start.22 = (bf16[128,128]{1,0:T(8,128)(2,1)}, bf16[128,128]{1,0:T(8,128)(2,1)S(1)}, u32[]{:S(2)}) copy-start(bf16[128,128]{1,0:T(8,128)(2,1)S(1)} %fusion.91) | copy-start | bytes 98308
  402.2 4.3 collective-permute-start
  407.1 163.9 %all-gather.14.cloned.1.call-start = ((), (), s32[]{:S(2)}) async-start(), calls=%async_computation.8 | async-start | bytes 1331200 | tf_op jit(solution)/shard_map/all_gather | solution.py:121
  485.5 2.3 copy-start.10
  572.3 1.6 copy-start.24
  592.5 34.1 %all-to-all-start.5 = ((f32[1,128,32]{2,0,1:T(1,128)}), f32[1,128,32]{2,0,1:T(1,128)S(1)}, u32[]{:S(2)}, u32[]{:S(2)}) async-start(f32[1,128,32]{2,0,1:T(1,128)} %bitcast.95), calls=%async_computation.5 | async-start | bytes 131072 | tf_op jit(solution)/shard_map/all_to_all | solution.py:140
  626.6 14.3 %all-to-all-start.4 = ((f32[1,128,32]{2,0,1:T(1,128)}), f32[1,128,32]{2,0,1:T(1,128)S(1)}, u32[]{:S(2)}, u32[]{:S(2)}) async-start(f32[1,128,32]{2,0,1:T(1,128)} %bitcast.92), calls=%async_computation.4 | async-start | bytes 131072 | tf_op jit(solution)/shard_map/all_to_all | solution.py:139
  640.9 57.1 %all-to-all-start.3 = ((f32[1,128,4096]{2,0,1:T(1,128)}), f32[1,128,4096]{2,0,1:T(1,128)S(1)}, u32[]{:S(2)}, u32[]{:S(2)}) async-start(f32[1,128,4096]{2,0,1:T(1,128)} %broadcast_in_dim.172), calls=%async_computation.3 | async-start | bytes 4194304 | tf_op jit(solution)/shard_map/all_to_all | solution.py:141
  646.8 136.1 %all-gather.20.cloned.1.call-start = ((), (), s32[]{:S(2)}) async-start(), calls=%async_computation.11 | async-start | bytes 1064960 | tf_op jit(solution)/shard_map/all_gather | solution.py:145
  702.9 81.5 %copy-start.8 = (bf16[1,4096,128]{2,1,0:T(8,128)(2,1)S(1)}, bf16[1,4096,128]{2,1,0:T(8,128)(2,1)}, u32[]{:S(2)}) copy-start(bf16[1,4096,128]{2,1,0:T(8,128)(2,1)} %param.28) | copy-start | bytes 3145732
  702.9 81.5 %copy-start.15 = (bf16[128,128]{1,0:T(8,128)(2,1)S(1)}, bf16[128,128]{1,0:T(8,128)(2,1)}, u32[]{:S(2)}) copy-start(bf16[128,128]{1,0:T(8,128)(2,1)} %bitcast_select_fusion) | copy-start | bytes 98308
  703.6 81.2 %copy-start.23 = (bf16[128,128]{1,0:T(8,128)(2,1)S(1)}, bf16[128,128]{1,0:T(8,128)(2,1)}, u32[]{:S(2)}) copy-start(bf16[128,128]{1,0:T(8,128)(2,1)} %copy-done.22) | copy-start | bytes 98308
  703.6 81.8 %copy-start.1 = (bf16[1,8192,80]{1,2,0:T(8,128)(2,1)S(1)}, bf16[1,8192,80]{1,2,0:T(8,128)(2,1)}, u32[]{:S(2)}) copy-start(bf16[1,8192,80]{1,2,0:T(8,128)(2,1)} %param.27) | copy-start | bytes 3932164
Sparse Core Ops, SparseCore 0:
  10.5 83.1 all-gather.15
  97.7 81.4 all-gather.9
  321.1 79.0 all-gather.17
  407.2 78.1 all-gather.11
  489.5 81.4 all-gather.13
  703.7 79.1 all-gather.19
where the time goes:
time: 800 us; the launch traced here: 793 us
  waiting for transfers between devices  610 us (76%)
  starting transfers between devices  74.2 us (9%)
  local copies, waits for them, and re-layouts  35 us (4%)
  matrix products  26.5 us (3%)
  other arithmetic  22.1 us (3%)
  between operations  16.8 us (2%)
  loops' own time  8.38 us (1%)
    all_gather x2, waiting for transfers between devices, on_device(): gathered = lax.all_gather(current, 'kv', axis=1, tiled=True)  164 us
    all_gather x2, waiting for transfers between devices, on_device(): lax.all_gather(attended, 'kv', axis=0, tiled=True)  158 us
    all_gather x2, waiting for transfers between devices, on_device(): united = lax.all_gather(local_cols, 'kv', axis=1, tiled=True)  157 us
    all_to_all x2, waiting for transfers between devices, on_device(): lax.all_to_all(partial_value[2][None], 'kv', split_axis=1, concat_axis=0,...  100 us
    all_to_all x2, starting transfers between devices, on_device(): lax.all_to_all(partial_value[1][None], 'kv', split_axis=1, concat_axis=0,...  49.9 us
    all_to_all x2, waiting for transfers between devices, on_device(): lax.all_to_all(partial_value[1][None], 'kv', split_axis=1, concat_axis=0,...  18.3 us
  transfers between devices with their start and end apart: 13, of which 13 were waited for; matrix products, arithmetic and copies ran while one was open for 2% of the time, Pallas kernels for 0%

commit v1 on v0

--- a/solution.py
+++ b/solution.py
@@ -6,6 +6,12 @@
 HD = 128
 HEADS_Q = 32
 KV_HEADS = 4
+
+
+def tiled_gather(x, axis, dim):
+    peers = lax.axis_size(axis)
+    repeats = [peers if d == dim else 1 for d in range(x.ndim)]
+    return lax.all_to_all(jnp.tile(x, repeats), axis, split_axis=dim, concat_axis=dim, tiled=True)
 
 
 def passed_along(block, axis, distance):
@@ -110,7 +116,7 @@
             block_starts[jnp.maximum(anchor, 0)],
             fresh_starts[jnp.clip(-anchor - 1, 0, tick_count - 2)],
         )
-        gathered = lax.all_gather(current, "kv", axis=1, tiled=True)
+        gathered = tiled_gather(current, "kv", 1)
         wide = gathered.astype(jnp.float32)
         normed = (
             wide * lax.rsqrt(jnp.mean(wide * wide, axis=1, keepdims=True) + 1e-05) * gain

time: 800 us -> 765 us (0.956)
  waiting for transfers between devices: 610 us -> 445 us
  blocking collectives: 0 us -> 122 us
  local copies, waits for them, and re-layouts: 35 us -> 43.3 us
    all_gather x2 -> x0, waiting for transfers between devices: 164 us -> none  [on_device(): gathered = lax.all_gather(current, 'kv', axis=1, tiled=True)]
    all_to_all x0 -> x2, blocking collectives: none -> 122 us  [tiled_gather(): lax.all_to_all(jnp.tile(x, repeats), axis, split_axis=dim, concat_axis=di...]
  transfers between devices with their start and end apart: 13 -> 11, of which waited for: 13 -> 11; matrix products, arithmetic and copies ran while one was open for 2% -> 2% of each run, Pallas kernels for 0% -> 0%
where the time goes in v1:
time: 765 us; the launch traced here: 756 us
  waiting for transfers between devices  445 us (58%)
  blocking collectives  122 us (16%)
  starting transfers between devices  73 us (10%)
  local copies, waits for them, and re-layouts  43.3 us (6%)
  matrix products  25.5 us (3%)
  other arithmetic  22.2 us (3%)
  between operations  16.5 us (2%)
  loops' own time  9.15 us (1%)
    all_gather x2, waiting for transfers between devices, on_device(): lax.all_gather(attended, 'kv', axis=0, tiled=True)  158 us
    all_gather x2, waiting for transfers between devices, on_device(): united = lax.all_gather(local_cols, 'kv', axis=1, tiled=True)  157 us
    all_to_all x2, blocking collectives, tiled_gather(): lax.all_to_all(jnp.tile(x, repeats), axis, split_axis=dim, concat_axis=di...  122 us
    all_to_all x2, waiting for transfers between devices, on_device(): lax.all_to_all(partial_value[2][None], 'kv', split_axis=1, concat_axis=0,...  100 us
    all_to_all x2, starting transfers between devices, on_device(): lax.all_to_all(partial_value[1][None], 'kv', split_axis=1, concat_axis=0,...  49 us
    all_to_all x2, waiting for transfers between devices, on_device(): lax.all_to_all(partial_value[1][None], 'kv', split_axis=1, concat_axis=0,...  18.3 us
  transfers between devices with their start and end apart: 11, of which 11 were waited for; matrix products, arithmetic and copies ran while one was open for 2% of the time, Pallas kernels for 0%

profile of v1, /device:TPU:1, one launch (start us, length us, event | category | flops | bytes accessed | tf_op | source)
XLA Modules:
  0.0 756.3 jit_solution(7747614661823505975)
XLA Ops:
  7.9 62.7 %all_to_all.84 = bf16[128,64,128]{2,0,1:T(8,128)(2,1)} all-to-all(bf16[128,64,128]{2,0,1:T(8,128)(2,1)S(1)} %tile.4), channel_id=1, replica_groups=mesh['section'=8,'kv'=64] {'kv'}, dimensions={1} | all-to-all | bytes 4194304 | tf_op jit(solution)/shard_map/all_to_all | solution.py:14
  70.6 3.2 copy.105
  83.7 76.3 %all-gather.7.cloned.1.call-done = bf16[128,5120]{0,1:T(8,128)(2,1)} async-done(((bf16[128,80]{0,1:T(8,128)(2,1)}), bf16[128,5120]{0,1:T(8,128)(2,1)}) %all-gather.7.cloned.1.call-update) | async-done | bytes 1310736 | tf_op jit(solution)/shard_map/all_gather | solution.py:127
  162.9 13.4 %while.58 = (s32[]{:T(128)}, f32[4,128,8]{1,2,0:T(8,128)S(1)}, f32[4,128,8]{1,2,0:T(8,128)S(1)}, f32[4,128,8,128]{3,1,2,0:T(8,128)S(1)}, bf16[4,128,8,128]{3,1,2...) while((s32[]{:T(128)}, f32[4,128,8]{1,2,0:T(8,128)S(1)}, ...), condition=%wide.region_4.5_spmd.clone, body=%wide.region_1.4_spmd.clone.sunk | while | flops 204863488 | bytes 5737833 | solution.py:50
  176.3 12.8 %conditional.2 = (f32[128,32]{0,1:T(8,128)S(1)}, f32[128,32]{0,1:T(8,128)S(1)}, f32[128,4096]{1,0:T(8,128)}) conditional(s32[]{:T(128)} %convert_element_type.63, (f32[128,4,8,128]{3,0,2,1:T(8,128)S(1)}, f32[128,32]{0,1:T(8,128)S(1)}, f32[128,32]{0,1:T(8,128)S(1)}) %tuple.196, (bf16[128,4096]{0,1:T(8,128)(2,1)}, bf16[128,5120]{0,1:T(8,128)(2,1)}, ...), branch_computations={%region_5.6_spmd, %region_6.11_spmd} | conditional | flops 69883904 | bytes 51759524 | solution.py:143
  177.6 2.9 copy.163
  189.9 24.9 %all-to-all-start.3 = ((f32[1,128,32]{2,0,1:T(1,128)}), f32[1,128,32]{2,0,1:T(1,128)S(1)}, u32[]{:S(2)}, u32[]{:S(2)}) async-start(f32[1,128,32]{2,0,1:T(1,128)} %bitcast.72), calls=%async_computation.3 | async-start | bytes 131072 | tf_op jit(solution)/shard_map/all_to_all | solution.py:146
  215.5 9.2 %all-to-all-done.3 = f32[1,128,32]{2,0,1:T(1,128)S(1)} async-done(((f32[1,128,32]{2,0,1:T(1,128)}), f32[1,128,32]{2,0,1:T(1,128)S(1)}, u32[]{:S(2)}, u32[]{:S(2)}) %all-to-all-start.3) | async-done | bytes 16416 | tf_op jit(solution)/shard_map/all_to_all | solution.py:146
  224.7 4.4 all-to-all-start.2
  229.1 5.3 broadcast_in_dim.169
  234.4 4.5 all-to-all-done.2
  239.0 5.9 all-to-all-start.1
  246.6 49.5 %all-to-all-done.1 = f32[1,128,4096]{2,0,1:T(1,128)S(1)} async-done(((f32[1,128,4096]{2,0,1:T(1,128)}), f32[1,128,4096]{2,0,1:T(1,128)S(1)}, u32[]{:S(2)}, u32[]{:S(2)}) %all-to-all-start.1) | async-done | bytes 2097184 | tf_op jit(solution)/shard_map/all_to_all | solution.py:147
  296.7 4.3 multiply_reduce_fusion.1
  301.7 79.2 %all-gather.11.cloned.1.call-done = bf16[64,2,4096]{2,1,0:T(2,128)(2,1)} async-done(((bf16[1,2,4096]{2,1,0:T(2,128)(2,1)}), bf16[64,2,4096]{2,1,0:T(2,128)(2,1)}) %all-gather.11.cloned.1.call-update) | async-done | bytes 1048592 | tf_op jit(solution)/shard_map/all_gather | solution.py:151
  382.9 3.3 collective-permute-start
  387.8 59.0 %all_to_all.85 = bf16[128,64,128]{2,0,1:T(8,128)(2,1)} all-to-all(bf16[128,64,128]{2,0,1:T(8,128)(2,1)S(1)} %tile.5), channel_id=1, replica_groups=mesh['section'=8,'kv'=64] {'kv'}, dimensions={1} | all-to-all | bytes 4194304 | tf_op jit(solution)/shard_map/all_to_all | solution.py:14
  446.8 3.2 copy.115
  453.8 81.2 %all-gather.9.cloned.1.call-done = bf16[128,5120]{0,1:T(8,128)(2,1)} async-done(((bf16[128,80]{0,1:T(8,128)(2,1)}), bf16[128,5120]{0,1:T(8,128)(2,1)}) %all-gather.9.cloned.1.call-update) | async-done | bytes 1310736 | tf_op jit(solution)/shard_map/all_gather | solution.py:127
  537.9 13.5 %while.59 = (s32[]{:T(128)}, f32[4,128,8]{1,2,0:T(8,128)S(1)}, f32[4,128,8]{1,2,0:T(8,128)S(1)}, f32[4,128,8,128]{3,1,2,0:T(8,128)S(1)}, bf16[4,128,8,128]{3,1,2...) while((s32[]{:T(128)}, f32[4,128,8]{1,2,0:T(8,128)S(1)}, ...), condition=%wide.region_18.19_spmd.clone, body=%wide.region_15.18_spmd.clone.sunk | while | flops 204863488 | bytes 5737833 | solution.py:50
  537.9 1.5 select_reduce_fusion.9
  551.4 4.4 conditional.3
  552.6 2.9 copy.164
  556.5 24.1 %all-to-all-start.7 = ((f32[1,128,32]{2,0,1:T(1,128)}), f32[1,128,32]{2,0,1:T(1,128)S(1)}, u32[]{:S(2)}, u32[]{:S(2)}) async-start(f32[1,128,32]{2,0,1:T(1,128)} %bitcast.95), calls=%async_computation.7 | async-start | bytes 131072 | tf_op jit(solution)/shard_map/all_to_all | solution.py:146
  581.4 9.2 %all-to-all-done.7 = f32[1,128,32]{2,0,1:T(1,128)S(1)} async-done(((f32[1,128,32]{2,0,1:T(1,128)}), f32[1,128,32]{2,0,1:T(1,128)S(1)}, u32[]{:S(2)}, u32[]{:S(2)}) %all-to-all-start.7) | async-done | bytes 16416 | tf_op jit(solution)/shard_map/all_to_all | solution.py:146
  590.5 4.4 all-to-all-start.6
  595.0 5.3 broadcast_in_dim.172
  600.3 4.5 all-to-all-done.6
  604.8 5.9 all-to-all-start.5
  611.0 50.9 %all-to-all-done.5 = f32[1,128,4096]{2,0,1:T(1,128)S(1)} async-done(((f32[1,128,4096]{2,0,1:T(1,128)}), f32[1,128,4096]{2,0,1:T(1,128)S(1)}, u32[]{:S(2)}, u32[]{:S(2)}) %all-to-all-start.5) | async-done | bytes 2097184 | tf_op jit(solution)/shard_map/all_to_all | solution.py:147
  662.5 4.3 multiply_reduce_fusion
  667.5 79.3 %all-gather.13.cloned.1.call-done = bf16[64,2,4096]{2,1,0:T(2,128)(2,1)} async-done(((bf16[1,2,4096]{2,1,0:T(2,128)(2,1)}), bf16[64,2,4096]{2,1,0:T(2,128)(2,1)}) %all-gather.13.cloned.1.call-update) | async-done | bytes 1048592 | tf_op jit(solution)/shard_map/all_gather | solution.py:151
  (125 shorter events, 59.2 us)
Async XLA Ops:
  6.5 69.9 %copy-start = (bf16[1,8192,80]{1,2,0:T(8,128)(2,1)S(1)}, bf16[1,8192,80]{1,2,0:T(8,128)(2,1)}, u32[]{:S(2)}) copy-start(bf16[1,8192,80]{1,2,0:T(8,128)(2,1)} %param.27) | copy-start | bytes 3932164
  6.5 153.5 %all-gather.7.cloned.1.call-start = ((), (), s32[]{:S(2)}) async-start(), calls=%async_computation.8 | async-start | bytes 1331200 | tf_op jit(solution)/shard_map/all_gather | solution.py:127
  73.8 1.1 copy-start.21
  76.4 1.2 copy-start.11
  76.5 2.4 copy-start.12
  77.6 3.6 copy-start.27
  161.3 1.4 copy-start.2
  189.9 34.8 %all-to-all-start.3 = ((f32[1,128,32]{2,0,1:T(1,128)}), f32[1,128,32]{2,0,1:T(1,128)S(1)}, u32[]{:S(2)}, u32[]{:S(2)}) async-start(f32[1,128,32]{2,0,1:T(1,128)} %bitcast.72), calls=%async_computation.3 | async-start | bytes 131072 | tf_op jit(solution)/shard_map/all_to_all | solution.py:146
  224.7 9.7 %copy-start.15 = (f32[1,128,32]{2,0,1:T(1,128)}, f32[1,128,32]{2,0,1:T(1,128)S(1)}, u32[]{:S(2)}) copy-start(f32[1,128,32]{2,0,1:T(1,128)S(1)} %all-to-all-done.3) | copy-start | bytes 49156
  224.7 14.3 %all-to-all-start.2 = ((f32[1,128,32]{2,0,1:T(1,128)}), f32[1,128,32]{2,0,1:T(1,128)S(1)}, u32[]{:S(2)}, u32[]{:S(2)}) async-start(f32[1,128,32]{2,0,1:T(1,128)} %bitcast.69), calls=%async_computation.2 | async-start | bytes 131072 | tf_op jit(solution)/shard_map/all_to_all | solution.py:145
  239.0 57.1 %all-to-all-start.1 = ((f32[1,128,4096]{2,0,1:T(1,128)}), f32[1,128,4096]{2,0,1:T(1,128)S(1)}, u32[]{:S(2)}, u32[]{:S(2)}) async-start(f32[1,128,4096]{2,0,1:T(1,128)} %broadcast_in_dim.169), calls=%async_computation.1 | async-start | bytes 4194304 | tf_op jit(solution)/shard_map/all_to_all | solution.py:147
  244.9 136.1 %all-gather.11.cloned.1.call-start = ((), (), s32[]{:S(2)}) async-start(), calls=%async_computation.10 | async-start | bytes 1064960 | tf_op jit(solution)/shard_map/all_gather | solution.py:151
  301.0 81.5 %copy-start.7 = (bf16[1,4096,128]{2,1,0:T(8,128)(2,1)S(1)}, bf16[1,4096,128]{2,1,0:T(8,128)(2,1)}, u32[]{:S(2)}) copy-start(bf16[1,4096,128]{2,1,0:T(8,128)(2,1)} %param.28) | copy-start | bytes 3145732
  301.0 81.5 %copy-start.20 = (bf16[1,128,128]{2,1,0:T(8,128)(2,1)S(1)}, bf16[1,128,128]{2,1,0:T(8,128)(2,1)}, u32[]{:S(2)}) copy-start(bf16[1,128,128]{2,1,0:T(8,128)(2,1)} %param.22) | copy-start | bytes 98308
  301.7 85.5 %copy-start.26 = (bf16[1,128,128]{2,1,0:T(8,128)(2,1)S(1)}, bf16[1,128,128]{2,1,0:T(8,128)(2,1)}, u32[]{:S(2)}) copy-start(bf16[1,128,128]{2,1,0:T(8,128)(2,1)} %param.23) | copy-start | bytes 98308
  301.7 233.4 %all-gather.9.cloned.1.call-start = ((), (), s32[]{:S(2)}) async-start(), calls=%async_computation.9 | async-start | bytes 1331200 | tf_op jit(solution)/shard_map/all_gather | solution.py:127
  382.9 64.0 %copy-start.23 = (bf16[128,128]{1,0:T(8,128)(2,1)}, bf16[128,128]{1,0:T(8,128)(2,1)S(1)}, u32[]{:S(2)}) copy-start(bf16[128,128]{1,0:T(8,128)(2,1)S(1)} %fusion.84) | copy-start | bytes 98308
  382.9 4.3 collective-permute-start
  387.2 0.6 copy-start.13
  450.1 1.1 copy-start.22
  536.3 1.6 copy-start.25
  556.5 34.0 %all-to-all-start.7 = ((f32[1,128,32]{2,0,1:T(1,128)}), f32[1,128,32]{2,0,1:T(1,128)S(1)}, u32[]{:S(2)}, u32[]{:S(2)}) async-start(f32[1,128,32]{2,0,1:T(1,128)} %bitcast.95), calls=%async_computation.7 | async-start | bytes 131072 | tf_op jit(solution)/shard_map/all_to_all | solution.py:146
  590.5 14.3 %all-to-all-start.6 = ((f32[1,128,32]{2,0,1:T(1,128)}), f32[1,128,32]{2,0,1:T(1,128)S(1)}, u32[]{:S(2)}, u32[]{:S(2)}) async-start(f32[1,128,32]{2,0,1:T(1,128)} %bitcast.92), calls=%async_computation.6 | async-start | bytes 131072 | tf_op jit(solution)/shard_map/all_to_all | solution.py:145
  604.8 57.1 %all-to-all-start.5 = ((f32[1,128,4096]{2,0,1:T(1,128)}), f32[1,128,4096]{2,0,1:T(1,128)S(1)}, u32[]{:S(2)}, u32[]{:S(2)}) async-start(f32[1,128,4096]{2,0,1:T(1,128)} %broadcast_in_dim.172), calls=%async_computation.5 | async-start | bytes 4194304 | tf_op jit(solution)/shard_map/all_to_all | solution.py:147
  610.7 136.1 %all-gather.13.cloned.1.call-start = ((), (), s32[]{:S(2)}) async-start(), calls=%async_computation.11 | async-start | bytes 1064960 | tf_op jit(solution)/shard_map/all_gather | solution.py:151
  666.8 81.4 %copy-start.8 = (bf16[1,4096,128]{2,1,0:T(8,128)(2,1)S(1)}, bf16[1,4096,128]{2,1,0:T(8,128)(2,1)}, u32[]{:S(2)}) copy-start(bf16[1,4096,128]{2,1,0:T(8,128)(2,1)} %param.28) | copy-start | bytes 3145732
  666.8 81.4 %copy-start.14 = (bf16[128,128]{1,0:T(8,128)(2,1)S(1)}, bf16[128,128]{1,0:T(8,128)(2,1)}, u32[]{:S(2)}) copy-start(bf16[128,128]{1,0:T(8,128)(2,1)} %copy-done.13) | copy-start | bytes 98308
  667.5 81.2 %copy-start.24 = (bf16[128,128]{1,0:T(8,128)(2,1)S(1)}, bf16[128,128]{1,0:T(8,128)(2,1)}, u32[]{:S(2)}) copy-start(bf16[128,128]{1,0:T(8,128)(2,1)} %copy-done.23) | copy-start | bytes 98308
  667.5 81.8 %copy-start.1 = (bf16[1,8192,80]{1,2,0:T(8,128)(2,1)S(1)}, bf16[1,8192,80]{1,2,0:T(8,128)(2,1)}, u32[]{:S(2)}) copy-start(bf16[1,8192,80]{1,2,0:T(8,128)(2,1)} %param.27) | copy-start | bytes 3932164
Sparse Core Ops, SparseCore 0:
  77.8 82.1 all-gather.6
  301.8 79.1 all-gather.10
  454.0 81.0 all-gather.8
  667.6 79.1 all-gather.12
